TPU v7x, 128 devices: a whole 4x4x4 slice. The times are simulated.
128 devices in a mesh: seq: 32 (over x, z, core), mp: 4 (over y).
Axes of the slice: x: 4, y: 4, z: 4, core: 2. Of those that a mesh axis runs over, the one named last changes fastest.
Arguments:
- hidden: bfloat16 [16384, 4096], P('seq', 'mp'), may hold values from -6 to 6
- w_zx: bfloat16 [4096, 2, 4096], P(None, None, 'mp'), may hold values from -0.09375 to 0.09375
- w_bc: bfloat16 [4096, 2, 512], P(None, None, 'mp'), may hold values from -0.09375 to 0.09375
- w_dt: bfloat16 [4096, 64], P(None, 'mp'), may hold values from -0.09375 to 0.09375
- conv_x: float32 [4, 4096], P(None, 'mp'), may hold values from -3 to 3
- conv_x_bias: float32 [4096], P('mp'), may hold values from -3 to 3
- conv_bc: float32 [4, 2, 512], P(None, None, 'mp'), may hold values from -3 to 3
- conv_bc_bias: float32 [2, 512], P(None, 'mp'), may hold values from -3 to 3
- a_log: float32 [64], P('mp'), may hold values from -9.5 to -0.5
- dt_bias: float32 [64], P('mp'), may hold values from -4 to -1
- d_skip: float32 [64], P('mp'), may hold values from 0.5 to 4
- norm_gain: float32 [4096], P('mp'), may hold values from 0.4 to 1.6
- state_bank: float32 [2, 64, 64, 128], P(None, 'mp'), may hold values from -2 to 2
- conv_bank_x: bfloat16 [2, 3, 4096], P(None, None, 'mp'), may hold values from -5 to 5
- conv_bank_bc: bfloat16 [2, 3, 2, 512], P(None, None, None, 'mp'), may hold values from -5 to 5
- prompt_blocks: int32 [9], replicated, may hold values from 1 to 48, 64 in all
- prompt_order: int32 [9], replicated, may hold values from 0 to 8, each once
- resume_slot: int32 [9], replicated, may hold values from 0 to 2
Outputs:
- mixed: bfloat16 [16384, 4096], P('seq', 'mp')
Inputs may be any that keep to these rules, and one draw needn't show every extreme that they name: `prompt_blocks`: blocks of each prompt; they sum to 64 and the longest is exactly 48. `prompt_order`: A permutation of the prompts. `resume_slot`: 2 means a fresh start from zero state and zero convolution rows.
All inputs are finite; a program needn't handle non-finite values.
Results may differ from a plain program's by a relative error of at most 0.0068.
Values may be sent and summed in bfloat16 or wider, within the bound.
No kernel may reach another device: no remote copies, remote signals or barrier semaphores. Data moves between devices by JAX's collectives and lax.ppermute only.
A program may use at most 192 MiB of HBM per device.

v0:
```python
import jax
import jax.numpy as jnp
from jax import lax
from jax.sharding import PartitionSpec as P

WIDTH = 4096
HEAD_DIM = 64
STATE = 128
BLOCK = 256
KERNEL = 4
BANK = 2


def from_behind(value, axis, steps):
    count = lax.axis_size(axis)
    pairs = [(source, (source + steps) % count) for source in range(count)]
    return lax.ppermute(value, axis, pairs)


def combine(earlier, later):
    return (earlier[0] * later[0], later[0][:, None, None] * earlier[1] + later[1])


def per_device(
    hidden,
    w_zx,
    w_bc,
    w_dt,
    conv_x,
    conv_x_bias,
    conv_bc,
    conv_bc_bias,
    a_log,
    dt_bias,
    d_skip,
    norm_gain,
    state_bank,
    conv_bank_x,
    conv_bank_bc,
    prompt_blocks,
    prompt_order,
    resume_slot,
):
    devices = lax.axis_size("seq")
    place = lax.axis_index("seq")
    rows_dev = hidden.shape[0]
    blocks = rows_dev // BLOCK
    inner_dev = w_zx.shape[2]
    gstate_dev = w_bc.shape[2]
    heads_dev = w_dt.shape[1]
    groups_dev = gstate_dev // STATE
    per_group = heads_dev // groups_dev
    channels = inner_dev + 2 * gstate_dev
    prompts = prompt_blocks.shape[0]
    flat_zx = w_zx.reshape(WIDTH, 2 * inner_dev)
    flat_bc = w_bc.reshape(WIDTH, 2 * gstate_dev)
    piece = lax.all_gather(hidden, "mp", axis=1, tiled=True)
    zx_sum = jnp.dot(piece, flat_zx, preferred_element_type=jnp.float32)
    bc_sum = jnp.dot(piece, flat_bc, preferred_element_type=jnp.float32)
    dt_raw = jnp.dot(piece, w_dt, preferred_element_type=jnp.float32)
    zx = zx_sum.astype(jnp.bfloat16)
    bc = bc_sum.astype(jnp.bfloat16)
    gate = zx[:, :inner_dev]
    mixin = jnp.concatenate([zx[:, inner_dev:], bc], axis=1).reshape(blocks, BLOCK, channels)
    own_tails = mixin[:, BLOCK - (KERNEL - 1) :, :]
    arrived = from_behind(own_tails, "seq", 1)
    wrapped = jnp.concatenate([jnp.zeros_like(arrived[:1]), arrived[:-1]], axis=0)
    before = jnp.where(place > 0, arrived, wrapped)
    prompt_ids = jnp.arange(prompts, dtype=jnp.int32)
    order_hot = (prompt_order[:, None] == prompt_ids[None, :]).astype(jnp.int32)
    lengths = jnp.sum(order_hot * prompt_blocks[None, :], axis=1)
    slots = jnp.sum(order_hot * resume_slot[None, :], axis=1)
    ends = jnp.cumsum(lengths)
    starts = ends - lengths
    stream_ids = jnp.arange(blocks, dtype=jnp.int32) * devices + place
    inside = (
        (stream_ids[:, None] >= starts[None, :]) & (stream_ids[:, None] < ends[None, :])
    ).astype(jnp.int32)
    block_slot = jnp.sum(inside * slots[None, :], axis=1)
    first = jnp.any(stream_ids[:, None] == starts[None, :], axis=1)
    pick = (block_slot[:, None] == jnp.arange(BANK, dtype=jnp.int32)[None, :]).astype(jnp.float32)
    bank_state = jnp.einsum("cr,rhpn->chpn", pick, state_bank, precision=lax.Precision.HIGHEST)
    bank_rows = jnp.concatenate(
        [conv_bank_x, conv_bank_bc.reshape(BANK, KERNEL - 1, 2 * gstate_dev)], axis=2
    )
    bank_tail = jnp.einsum("cr,rkz->ckz", pick, bank_rows.astype(jnp.float32)).astype(jnp.bfloat16)
    tail = jnp.where(first[:, None, None], bank_tail, before)
    kernel = jnp.concatenate([conv_x, conv_bc.reshape(KERNEL, 2 * gstate_dev)], axis=1)
    bias = jnp.concatenate([conv_x_bias, conv_bc_bias.reshape(2 * gstate_dev)], axis=0)
    padded = jnp.concatenate([tail, mixin], axis=1).astype(jnp.float32)
    acc = bias[None, None, :] + padded[:, 0:BLOCK] * kernel[0]
    for k in range(1, KERNEL):
        acc = acc + padded[:, k : k + BLOCK] * kernel[k]
    conv = jax.nn.silu(acc).astype(jnp.bfloat16)
    xs = conv[..., :inner_dev].reshape(blocks, BLOCK, groups_dev, per_group, HEAD_DIM)
    bs = conv[..., inner_dev : inner_dev + gstate_dev].reshape(blocks, BLOCK, groups_dev, STATE)
    cq = conv[..., inner_dev + gstate_dev :].reshape(blocks, BLOCK, groups_dev, STATE)
    dt = jax.nn.softplus(dt_raw.reshape(blocks, BLOCK, heads_dev) + dt_bias[None, None, :])
    cum = jnp.cumsum(dt * (-jnp.exp(a_log))[None, None, :], axis=1)
    scores = jnp.einsum("cqgn,ckgn->cgqk", cq, bs, preferred_element_type=jnp.float32)
    cum_h = cum.transpose(0, 2, 1)
    lower = jnp.arange(BLOCK)[:, None] >= jnp.arange(BLOCK)[None, :]
    damp = jnp.exp(
        jnp.where(lower[None, None], cum_h[:, :, :, None] - cum_h[:, :, None, :], -jnp.inf)
    )
    damp = damp.reshape(blocks, groups_dev, per_group, BLOCK, BLOCK)
    dt_h = dt.transpose(0, 2, 1).reshape(blocks, groups_dev, per_group, 1, BLOCK)
    mix = (scores[:, :, None] * damp * dt_h).astype(jnp.bfloat16)
    y_intra = jnp.einsum("cgjqk,ckgjp->cqgjp", mix, xs, preferred_element_type=jnp.float32)
    last = cum[:, -1, :]
    grow = jnp.exp(last)
    factor = (dt * jnp.exp(last[:, None, :] - cum)).reshape(blocks, BLOCK, groups_dev, per_group, 1)
    weighted = (xs.astype(jnp.float32) * factor).astype(jnp.bfloat16)
    local_state = jnp.einsum(
        "cqgjp,cqgn->cgjpn", weighted, bs, preferred_element_type=jnp.float32
    ).reshape(blocks, heads_dev, HEAD_DIM, STATE)
    step_a = jnp.where(first[:, None], 0.0, grow)
    step_b = local_state + jnp.where(
        first[:, None, None, None], grow[:, :, None, None] * bank_state, 0.0
    )
    core = place % 2
    chip = place // 2
    chips = devices // 2
    half = heads_dev // 2
    rows = blocks * half

    def keep(part, at):
        piece = lax.dynamic_slice_in_dim(part, at * half, half, axis=1)
        return piece.reshape((rows,) + part.shape[2:])

    pair = [(source, source ^ 1) for source in range(devices)]
    mine = (keep(step_a, core), keep(step_b, core))
    got = lax.ppermute((keep(step_a, 1 - core), keep(step_b, 1 - core)), "seq", pair)
    early = jax.tree.map(lambda own, other: jnp.where(core == 0, own, other), mine, got)
    later = jax.tree.map(lambda own, other: jnp.where(core == 0, other, own), mine, got)
    quarter = half // 2
    split_heads = lambda part: [
        part.reshape((blocks, 2, quarter) + part.shape[1:])[:, g].reshape(
            (blocks * quarter,) + part.shape[1:]
        )
        for g in range(2)
    ]
    chip_a, chip_b = combine(early, later)
    lanes = [list(pair) for pair in zip(split_heads(chip_a), split_heads(chip_b))]
    priors = [[jnp.ones_like(lane[0]), jnp.zeros_like(lane[1])] for lane in lanes]

    def wrap(part, neutral, late):
        moved = jnp.concatenate(
            [jnp.full_like(part[:quarter], neutral), part[: part.shape[0] - quarter]], axis=0
        )
        return jnp.where(late, part, moved)

    span = 1
    while span < chips:
        late = chip >= span
        for g in range(2):
            got_a, got_b = from_behind(tuple(lanes[g]), "seq", 2 * span)
            lead = (wrap(got_a, 1.0, late), wrap(got_b, 0.0, late))
            lanes[g] = list(combine(lead, tuple(lanes[g])))
            priors[g] = list(combine(lead, tuple(priors[g])))
        span *= 2
    joined = []
    for g in range(2):
        run_a, run_b = lanes[g]
        prior_a, prior_b = priors[g]
        lift = combine((run_a[:quarter], run_b[:quarter]), (prior_a[quarter:], prior_b[quarter:]))[
            1
        ]
        joined.append(jnp.concatenate([prior_b[:quarter], lift], axis=0))
    before_chip = jnp.concatenate(
        [part.reshape((blocks, quarter) + part.shape[1:]) for part in joined], axis=1
    ).reshape(chip_b.shape)
    after_early = early[0][:, None, None] * before_chip + early[1]
    own_part = jnp.where(core == 0, before_chip, after_early)
    other_part = lax.ppermute(jnp.where(core == 0, after_early, before_chip), "seq", pair)
    split_rows = lambda part: part.reshape((blocks, half) + part.shape[1:])
    own_part, other_part = (split_rows(own_part), split_rows(other_part))
    previous = jnp.where(
        core == 0,
        jnp.concatenate([own_part, other_part], axis=1),
        jnp.concatenate([other_part, own_part], axis=1),
    )
    state_in = jnp.where(first[:, None, None, None], bank_state, previous)
    read = jnp.einsum(
        "cqgn,cgjpn->cqgjp",
        cq.astype(jnp.float32),
        state_in.reshape(blocks, groups_dev, per_group, HEAD_DIM, STATE),
        precision=lax.Precision.HIGHEST,
    )
    growth = jnp.exp(cum).reshape(blocks, BLOCK, groups_dev, per_group, 1)
    skip = d_skip.reshape(1, 1, groups_dev, per_group, 1)
    y_total = y_intra + growth * read + skip * xs.astype(jnp.float32)
    gated = y_total.reshape(rows_dev, inner_dev) * jax.nn.silu(gate.astype(jnp.float32))
    grouped = gated.reshape(rows_dev, groups_dev, inner_dev // groups_dev)
    scale = lax.rsqrt(jnp.mean(grouped * grouped, axis=2, keepdims=True) + 1e-05)
    result = (grouped * scale).reshape(rows_dev, inner_dev) * norm_gain[None, :]
    return result.astype(jnp.bfloat16)


def solution(mesh):
    placed = (
        P("seq", "mp"),
        P(None, None, "mp"),
        P(None, None, "mp"),
        P(None, "mp"),
        P(None, "mp"),
        P("mp"),
        P(None, None, "mp"),
        P(None, "mp"),
        P("mp"),
        P("mp"),
        P("mp"),
        P("mp"),
        P(None, "mp", None, None),
        P(None, None, "mp"),
        P(None, None, None, "mp"),
        P(),
        P(),
        P(),
    )
    return jax.shard_map(
        per_device, mesh=mesh, in_specs=placed, out_specs=P("seq", "mp"), check_vma=False
    )
```

profile of v0, /device:TPU:1, one launch (start us, length us, event | category | flops | bytes accessed | tf_op | source)
XLA Modules:
  0.0 195.6 jit_solution(3872452470648923946)
XLA Ops:
  8.4 17.2 %copy.111 = bf16[512,8,2,1024]{3,1,2,0:T(8,128)(2,1)} copy(bf16[512,8,2,1024]{3,2,1,0:T(2,128)(2,1)} %bitcast.142) | data formatting | bytes 33554432
  26.2 34.1 %all-gather.2.cloned.1.call-done = bf16[512,4096]{1,0:T(8,128)(2,1)} async-done(((bf16[512,1024]{1,0:T(8,128)(2,1)}), bf16[512,4096]{1,0:T(8,128)(2,1)}) %all-gather.2.cloned.1.call-update) | async-done | bytes 4194320 | tf_op jit(solution)/shard_map/all_gather | solution.py:57
  60.3 15.8 %convolution_convert_fusion = bf16[512,2048]{1,0:T(8,128)(2,1)S(1)} fusion(bf16[512,4096]{1,0:T(8,128)(2,1)} %all-gather.2.cloned.1.call-done, bf16[4096,2048]{1,0:T(8,128)(2,1)} %bitcast.143), kind=kOutput, calls=%fused_computation.8 | convolution fusion | flops 8590983168 | bytes 23068672 | tf_op jit(solution)/shard_map/dot_general | solution.py:58
  76.2 2.2 %copy-done.16 = bf16[4096,2,128]{2,1,0:T(2,128)(2,1)S(1)} copy-done((bf16[4096,2,128]{2,1,0:T(2,128)(2,1)S(1)}, bf16[4096,2,128]{2,1,0:T(2,128)(2,1)}, u32[]{:S(2)}) %copy-start.16) | copy-done | bytes 2097176
  79.9 2.1 %collective-permute-start = (bf16[2,3,1280]{2,0,1:T(2,128)(2,1)S(1)}, bf16[2,3,1280]{2,0,1:T(2,128)(2,1)S(1)}, u32[]{:S(2)}, u32[]{:S(2)}) collective-permute-start(bf16[2,3,1280]{2,0,1:T(2,128)(2,1)S(1)} %copy.107), channel_id=1, source_target_pairs={{0,4},{4,8},{8,12},{12,16},{16,20},{20,24},{24,28},{28,32},{32,36}... | collective-permute-start | bytes 46088 | tf_op jit(solution)/shard_map/ppermute | solution.py:17
  89.5 1.7 multiply_convert_fusion.2
  91.2 1.4 slice_convert_fusion
  92.6 2.3 %copy.84 = bf16[2,256,1024]{1,2,0:T(8,128)(2,1)} copy(bf16[2,256,1024]{2,1,0:T(8,128)(2,1)} %get-tuple-element.33) | data formatting | bytes 2097152 | tf_op jit(solution)/shard_map/slice | solution.py:95
  94.9 1.7 fusion.23
  96.6 4.6 %copy_add_fusion = (f32[2,16,64,128]{3,0,2,1:T(2,128)S(1)}, f32[2,16,64,128]{3,0,2,1:T(2,128)}) fusion(f32[2,16,64,128]{3,2,1,0:T(8,128)S(1)} %fusion.23, pred[2]{0:T(512)(128)(4,1)S(1)} %compare_reduce_fusion, f32[2,16]{0,1:T(8,128)S(1)} %copy.89, f32[2,16,64,128]{3,2,1,0:T(8,128)S(1)} %copy-done, s32[2]{0:T(128)S(1)} %fusion.46), kind=kOutput, calls=%fused_computation.42 | convolution fusion | flops 7077892 | bytes 4194442 | tf_op jit(solution)/shard_map/cr,rhpn->chpn/dot_general | solution.py:82
  102.2 2.5 %collective-permute-start.3 = (f32[8]{0:T(128)S(1)}, f32[8]{0:T(128)S(1)}, u32[]{:S(2)}, u32[]{:S(2)}) collective-permute-start(f32[8]{0:T(128)S(1)} %get-tuple-element.18), channel_id=1, source_target_pairs={{0,16},{4,20},{8,24},{12,28},{16,32},{20,36},{24,40},{28,44},{32,4... | collective-permute-start | bytes 104 | tf_op jit(solution)/shard_map/ppermute | solution.py:17
  104.8 1.4 collective-permute-start.12
  106.2 2.1 %collective-permute-done.3 = f32[8]{0:T(128)S(1)} collective-permute-done((f32[8]{0:T(128)S(1)}, f32[8]{0:T(128)S(1)}, u32[]{:S(2)}, u32[]{:S(2)}) %collective-permute-start.3) | collective-permute-done | bytes 64 | tf_op jit(solution)/shard_map/ppermute | solution.py:17
  112.0 1.6 collective-permute-start.10
  113.6 4.8 %collective-permute-done.6 = f32[8,64,128]{2,1,0:T(8,128)S(1)} collective-permute-done((f32[8,64,128]{2,1,0:T(8,128)S(1)}, f32[8,64,128]{2,1,0:T(8,128)S(1)}, u32[]{:S(2)}, u32[]{:S(2)}) %collective-permute-start.6) | collective-permute-done | bytes 262176 | tf_op jit(solution)/shard_map/ppermute | solution.py:17
  119.8 4.0 %collective-permute-done.14 = f32[8,64,128]{2,1,0:T(8,128)S(1)} collective-permute-done((f32[8,64,128]{2,1,0:T(8,128)S(1)}, f32[8,64,128]{2,1,0:T(8,128)S(1)}, u32[]{:S(2)}, u32[]{:S(2)}) %collective-permute-start.14) | collective-permute-done | bytes 262176 | tf_op jit(solution)/shard_map/ppermute | solution.py:17
  124.2 4.8 %collective-permute-done.7 = f32[8,64,128]{2,1,0:T(8,128)S(1)} collective-permute-done((f32[8,64,128]{2,1,0:T(8,128)S(1)}, f32[8,64,128]{2,1,0:T(8,128)S(1)}, u32[]{:S(2)}, u32[]{:S(2)}) %collective-permute-start.7) | collective-permute-done | bytes 262176 | tf_op jit(solution)/shard_map/ppermute | solution.py:17
  129.3 5.3 %collective-permute-done.15 = f32[8,64,128]{2,1,0:T(8,128)S(1)} collective-permute-done((f32[8,64,128]{2,1,0:T(8,128)S(1)}, f32[8,64,128]{2,1,0:T(8,128)S(1)}, u32[]{:S(2)}, u32[]{:S(2)}) %collective-permute-start.15) | collective-permute-done | bytes 262176 | tf_op jit(solution)/shard_map/ppermute | solution.py:17
  135.7 1.4 collective-permute-start.9
  137.3 5.9 %collective-permute-done.16 = f32[8,64,128]{2,1,0:T(8,128)S(1)} collective-permute-done((f32[8,64,128]{2,1,0:T(8,128)S(1)}, f32[8,64,128]{2,1,0:T(8,128)S(1)}, u32[]{:S(2)}, u32[]{:S(2)}) %collective-permute-start.16) | collective-permute-done | bytes 262176 | tf_op jit(solution)/shard_map/ppermute | solution.py:17
  143.7 3.7 %collective-permute-done.9 = f32[8,64,128]{2,1,0:T(8,128)S(1)} collective-permute-done((f32[8,64,128]{2,1,0:T(8,128)S(1)}, f32[8,64,128]{2,1,0:T(8,128)S(1)}, u32[]{:S(2)}, u32[]{:S(2)}) %collective-permute-start.9) | collective-permute-done | bytes 262176 | tf_op jit(solution)/shard_map/ppermute | solution.py:17
  147.7 5.8 %collective-permute-done.17 = f32[8,64,128]{2,1,0:T(8,128)S(1)} collective-permute-done((f32[8,64,128]{2,1,0:T(8,128)S(1)}, f32[8,64,128]{2,1,0:T(8,128)S(1)}, u32[]{:S(2)}, u32[]{:S(2)}) %collective-permute-start.17) | collective-permute-done | bytes 262176 | tf_op jit(solution)/shard_map/ppermute | solution.py:17
  155.1 10.9 %collective-permute-start.19 = (f32[16,64,128]{2,1,0:T(8,128)}, f32[16,64,128]{2,1,0:T(8,128)}, u32[]{:S(2)}, u32[]{:S(2)}) collective-permute-start(f32[16,64,128]{2,1,0:T(8,128)} %get-tuple-element.31), channel_id=1, source_target_pairs={{0,4},{4,0},{8,12},{12,8},{16,20},{20,16},{24,28},{28,24},{32,36},... | collective-permute-start | bytes 1572872 | tf_op jit(solution)/shard_map/ppermute | solution.py:175
  166.0 1.8 copy.98
  169.2 1.4 copy.93
  170.6 1.4 copy.94
  173.0 2.1 %fusion.25 = f32[2,16,64,256]{3,2,1,0:T(8,128)S(1)} fusion(f32[2,16,64,128]{3,0,2,1:T(2,128)S(1)} %fusion.24, bf16[2,256,1280]{2,1,0:T(8,128)(2,1)} %copy-done.1), kind=kOutput, calls=%fused_computation.40 | convolution fusion | flops 805306368 | bytes 3276800 | tf_op jit(solution)/shard_map/cqgn,cgjpn->cqgjp/dot_general | solution.py:184
  175.0 2.6 %fusion.19 = f32[2,256,1,16,64]{1,4,3,0,2:T(8,128)S(1)} fusion(f32[2,16,64,256]{3,2,1,0:T(8,128)S(1)} %fusion.25, f32[2,256,1,16,64]{1,4,3,0,2:T(8,128)S(1)} %bitcast.149, bf16[2,256,16,64]{1,3,2,0:T(8,128)(2,1)S(1)} %bitcast.147, f32[2,16,256]{2,1,0:T(8,128)S(1)} %get-tuple-element.42, f32[2,16,256]{2,1,0:T(8,128)S(1)} %get-tuple-element.45, ...), kind=kOutput, calls=%fused_computation.30 | convolution fusion | flops 281018368 | bytes 8028224 | tf_op jit(solution)/shard_map/cgjqk,ckgjp->cqgjp/dot_general | solution.py:109
  177.7 3.8 %copy.105 = f32[2,256,1,16,64]{4,3,1,0,2:T(8,128)} copy(f32[2,256,1,16,64]{1,4,3,0,2:T(8,128)S(1)} %fusion.19) | data formatting | bytes 4194304 | tf_op jit(solution)/shard_map/reshape | solution.py:193
  181.5 3.5 %reshape.290 = f32[512,1024]{1,0:T(8,128)S(1)} reshape(f32[2,256,1,16,64]{4,3,1,0,2:T(8,128)} %copy.105) | data formatting | bytes 4194304 | tf_op jit(solution)/shard_map/reshape | solution.py:193
  185.0 2.1 %multiply_reduce_fusion = f32[512]{0:T(512)S(1)} fusion(f32[512,1024]{1,0:T(8,128)S(1)} %reshape.290, bf16[512,2048]{1,0:T(8,128)(2,1)} %copy-done.2), kind=kLoop, calls=%fused_computation.32 | loop fusion | flops 4193792 | bytes 3147776 | tf_op jit(solution)/shard_map/reduce_sum | solution.py:195
  187.1 1.7 multiply_convert_fusion.3
  (148 shorter events, 23.8 us)
Async XLA Ops:
  6.5 90.0 %copy-start = (f32[2,16,64,128]{3,2,1,0:T(8,128)S(1)}, f32[2,16,64,128]{3,2,1,0:T(8,128)}, u32[]{:S(2)}) copy-start(f32[2,16,64,128]{3,2,1,0:T(8,128)} %param.30) | copy-start | bytes 3145732
  6.5 53.7 %all-gather.2.cloned.1.call-start = ((), (), s32[]{:S(2)}) async-start(), calls=%async_computation | async-start | bytes 5242880 | tf_op jit(solution)/shard_map/all_gather | solution.py:57
  8.4 17.2 %copy-start.13 = (bf16[2,3,2,128]{3,2,1,0:T(2,128)(2,1)S(1)}, bf16[2,3,2,128]{3,2,1,0:T(2,128)(2,1)}, u32[]{:S(2)}) copy-start(bf16[2,3,2,128]{3,2,1,0:T(2,128)(2,1)} %param.32) | copy-start | bytes 9220
  8.4 17.3 %copy-start.11 = (f32[1024]{0:T(1024)S(1)}, f32[1024]{0:T(1024)}, u32[]{:S(2)}) copy-start(f32[1024]{0:T(1024)} %param.23) | copy-start | bytes 12292
  8.4 17.3 %copy-start.15 = (f32[2,128]{1,0:T(2,128)S(1)}, f32[2,128]{1,0:T(2,128)}, u32[]{:S(2)}) copy-start(f32[2,128]{1,0:T(2,128)} %param.25) | copy-start | bytes 3076
  8.4 17.3 %copy-start.9 = (f32[4,1024]{1,0:T(4,128)S(1)}, f32[4,1024]{1,0:T(4,128)}, u32[]{:S(2)}) copy-start(f32[4,1024]{1,0:T(4,128)} %param.22) | copy-start | bytes 49156
  8.4 17.7 %copy-start.12 = (f32[4,2,128]{2,1,0:T(2,128)S(1)}, f32[4,2,128]{2,1,0:T(2,128)}, u32[]{:S(2)}) copy-start(f32[4,2,128]{2,1,0:T(2,128)} %param.24) | copy-start | bytes 12292
  8.4 17.8 %copy-start.18 = (f32[16]{0:T(128)S(1)}, f32[16]{0:T(128)}, u32[]{:S(2)}) copy-start(f32[16]{0:T(128)} %param.26) | copy-start | bytes 196
  60.3 15.9 %copy-start.4 = (bf16[512,4096]{1,0:T(8,128)(2,1)S(1)}, bf16[512,4096]{1,0:T(8,128)(2,1)}, u32[]{:S(2)}) copy-start(bf16[512,4096]{1,0:T(8,128)(2,1)} %all-gather.2.cloned.1.call-done) | copy-start | bytes 12582916
  76.0 3.7 %copy-start.2 = (bf16[512,2048]{1,0:T(8,128)(2,1)}, bf16[512,2048]{1,0:T(8,128)(2,1)S(1)}, u32[]{:S(2)}) copy-start(bf16[512,2048]{1,0:T(8,128)(2,1)S(1)} %convolution_convert_fusion) | copy-start | bytes 6291460
  79.9 9.1 %copy-start.17 = (bf16[2,3,1024]{2,0,1:T(2,128)(2,1)S(1)}, bf16[2,3,1024]{2,0,1:T(2,128)(2,1)}, u32[]{:S(2)}) copy-start(bf16[2,3,1024]{2,0,1:T(2,128)(2,1)} %param.31) | copy-start | bytes 36868
  79.9 9.1 %collective-permute-start = (bf16[2,3,1280]{2,0,1:T(2,128)(2,1)S(1)}, bf16[2,3,1280]{2,0,1:T(2,128)(2,1)S(1)}, u32[]{:S(2)}, u32[]{:S(2)}) collective-permute-start(bf16[2,3,1280]{2,0,1:T(2,128)(2,1)S(1)} %copy.107), channel_id=1, source_target_pairs={{0,4},{4,8},{8,12},{12,16},{16,20},{20,24},{24,28},{28,32},{32,36}... | collective-permute-start | bytes 46088 | tf_op jit(solution)/shard_map/ppermute | solution.py:17
  85.3 1.2 collective-permute-start.1
  86.7 15.5 %collective-permute-start.2 = (f32[8]{0:T(128)S(1)}, f32[8]{0:T(128)S(1)}, u32[]{:S(2)}, u32[]{:S(2)}) collective-permute-start(f32[8]{0:T(128)S(1)} %reshape_squeeze.12), channel_id=1, source_target_pairs={{0,8},{4,12},{8,16},{12,20},{16,24},{20,28},{24,32},{28,36},{32,40... | collective-permute-start | bytes 104 | tf_op jit(solution)/shard_map/ppermute | solution.py:17
  88.0 16.7 %collective-permute-start.11 = (f32[8]{0:T(128)S(1)}, f32[8]{0:T(128)S(1)}, u32[]{:S(2)}, u32[]{:S(2)}) collective-permute-start(f32[8]{0:T(128)S(1)} %reshape_squeeze.14), channel_id=1, source_target_pairs={{0,8},{4,12},{8,16},{12,20},{16,24},{20,28},{24,32},{28,36},{32,40... | collective-permute-start | bytes 104 | tf_op jit(solution)/shard_map/ppermute | solution.py:17
  101.3 7.1 %collective-permute-start.5 = (f32[16,64,128]{2,1,0:T(8,128)S(1)}, f32[16,64,128]{2,1,0:T(8,128)S(1)}, u32[]{:S(2)}, u32[]{:S(2)}) collective-permute-start(f32[16,64,128]{2,1,0:T(8,128)S(1)} %bitcast.155), channel_id=1, source_target_pairs={{0,4},{4,0},{8,12},{12,8},{16,20},{20,16},{24,28},{28,24},{32,36},... | collective-permute-start | bytes 1572872 | tf_op jit(solution)/shard_map/ppermute | solution.py:133
  102.2 6.0 %collective-permute-start.3 = (f32[8]{0:T(128)S(1)}, f32[8]{0:T(128)S(1)}, u32[]{:S(2)}, u32[]{:S(2)}) collective-permute-start(f32[8]{0:T(128)S(1)} %get-tuple-element.18), channel_id=1, source_target_pairs={{0,16},{4,20},{8,24},{12,28},{16,32},{20,36},{24,40},{28,44},{32,4... | collective-permute-start | bytes 104 | tf_op jit(solution)/shard_map/ppermute | solution.py:17
  104.8 6.0 %collective-permute-start.12 = (f32[8]{0:T(128)S(1)}, f32[8]{0:T(128)S(1)}, u32[]{:S(2)}, u32[]{:S(2)}) collective-permute-start(f32[8]{0:T(128)S(1)} %get-tuple-element.25), channel_id=1, source_target_pairs={{0,16},{4,20},{8,24},{12,28},{16,32},{20,36},{24,40},{28,44},{32,4... | collective-permute-start | bytes 104 | tf_op jit(solution)/shard_map/ppermute | solution.py:17
  108.3 3.6 %collective-permute-start.4 = (f32[8]{0:T(128)S(1)}, f32[8]{0:T(128)S(1)}, u32[]{:S(2)}, u32[]{:S(2)}) collective-permute-start(f32[8]{0:T(128)S(1)} %fusion.58), channel_id=1, source_target_pairs={{0,32},{4,36},{8,40},{12,44},{16,48},{20,52},{24,56},{28,60},{32,6... | collective-permute-start | bytes 104 | tf_op jit(solution)/shard_map/ppermute | solution.py:17
  108.6 9.8 %collective-permute-start.6 = (f32[8,64,128]{2,1,0:T(8,128)S(1)}, f32[8,64,128]{2,1,0:T(8,128)S(1)}, u32[]{:S(2)}, u32[]{:S(2)}) collective-permute-start(f32[8,64,128]{2,1,0:T(8,128)S(1)} %bitcast.154), channel_id=1, source_target_pairs={{0,8},{4,12},{8,16},{12,20},{16,24},{20,28},{24,32},{28,36},{32,40... | collective-permute-start | bytes 786440 | tf_op jit(solution)/shard_map/ppermute | solution.py:17
  110.9 7.7 %collective-permute-start.13 = (f32[8]{0:T(128)S(1)}, f32[8]{0:T(128)S(1)}, u32[]{:S(2)}, u32[]{:S(2)}) collective-permute-start(f32[8]{0:T(128)S(1)} %fusion.60), channel_id=1, source_target_pairs={{0,32},{4,36},{8,40},{12,44},{16,48},{20,52},{24,56},{28,60},{32,6... | collective-permute-start | bytes 104 | tf_op jit(solution)/shard_map/ppermute | solution.py:17
  112.0 17.1 %collective-permute-start.10 = (f32[8]{0:T(128)S(1)}, f32[8]{0:T(128)S(1)}, u32[]{:S(2)}, u32[]{:S(2)}) collective-permute-start(f32[8]{0:T(128)S(1)} %fusion.53), channel_id=1, source_target_pairs={{0,64},{4,68},{8,72},{12,76},{16,80},{20,84},{24,88},{28,92},{32,9... | collective-permute-start | bytes 104 | tf_op jit(solution)/shard_map/ppermute | solution.py:17
  113.6 10.3 %collective-permute-start.14 = (f32[8,64,128]{2,1,0:T(8,128)S(1)}, f32[8,64,128]{2,1,0:T(8,128)S(1)}, u32[]{:S(2)}, u32[]{:S(2)}) collective-permute-start(f32[8,64,128]{2,1,0:T(8,128)S(1)} %bitcast.153), channel_id=1, source_target_pairs={{0,8},{4,12},{8,16},{12,20},{16,24},{20,28},{24,32},{28,36},{32,40... | collective-permute-start | bytes 786440 | tf_op jit(solution)/shard_map/ppermute | solution.py:17
  118.5 10.5 %collective-permute-start.7 = (f32[8,64,128]{2,1,0:T(8,128)S(1)}, f32[8,64,128]{2,1,0:T(8,128)S(1)}, u32[]{:S(2)}, u32[]{:S(2)}) collective-permute-start(f32[8,64,128]{2,1,0:T(8,128)S(1)} %multiply_add_fusion.5), channel_id=1, source_target_pairs={{0,16},{4,20},{8,24},{12,28},{16,32},{20,36},{24,40},{28,44},{32,4... | collective-permute-start | bytes 786440 | tf_op jit(solution)/shard_map/ppermute | solution.py:17
  118.7 18.4 %collective-permute-start.18 = (f32[8]{0:T(128)S(1)}, f32[8]{0:T(128)S(1)}, u32[]{:S(2)}, u32[]{:S(2)}) collective-permute-start(f32[8]{0:T(128)S(1)} %fusion.55), channel_id=1, source_target_pairs={{0,64},{4,68},{8,72},{12,76},{16,80},{20,84},{24,88},{28,92},{32,9... | collective-permute-start | bytes 104 | tf_op jit(solution)/shard_map/ppermute | solution.py:17
  124.0 10.6 %collective-permute-start.15 = (f32[8,64,128]{2,1,0:T(8,128)S(1)}, f32[8,64,128]{2,1,0:T(8,128)S(1)}, u32[]{:S(2)}, u32[]{:S(2)}) collective-permute-start(f32[8,64,128]{2,1,0:T(8,128)S(1)} %multiply_add_fusion.2), channel_id=1, source_target_pairs={{0,16},{4,20},{8,24},{12,28},{16,32},{20,36},{24,40},{28,44},{32,4... | collective-permute-start | bytes 786440 | tf_op jit(solution)/shard_map/ppermute | solution.py:17
  129.1 6.5 %collective-permute-start.8 = (f32[8,64,128]{2,1,0:T(8,128)S(1)}, f32[8,64,128]{2,1,0:T(8,128)S(1)}, u32[]{:S(2)}, u32[]{:S(2)}) collective-permute-start(f32[8,64,128]{2,1,0:T(8,128)S(1)} %multiply_add_fusion.4), channel_id=1, source_target_pairs={{0,32},{4,36},{8,40},{12,44},{16,48},{20,52},{24,56},{28,60},{32,6... | collective-permute-start | bytes 786440 | tf_op jit(solution)/shard_map/ppermute | solution.py:17
  134.7 8.6 %collective-permute-start.16 = (f32[8,64,128]{2,1,0:T(8,128)S(1)}, f32[8,64,128]{2,1,0:T(8,128)S(1)}, u32[]{:S(2)}, u32[]{:S(2)}) collective-permute-start(f32[8,64,128]{2,1,0:T(8,128)S(1)} %multiply_add_fusion.1), channel_id=1, source_target_pairs={{0,32},{4,36},{8,40},{12,44},{16,48},{20,52},{24,56},{28,60},{32,6... | collective-permute-start | bytes 786440 | tf_op jit(solution)/shard_map/ppermute | solution.py:17
  135.7 11.7 %collective-permute-start.9 = (f32[8,64,128]{2,1,0:T(8,128)S(1)}, f32[8,64,128]{2,1,0:T(8,128)S(1)}, u32[]{:S(2)}, u32[]{:S(2)}) collective-permute-start(f32[8,64,128]{2,1,0:T(8,128)S(1)} %multiply_add_fusion.3), channel_id=1, source_target_pairs={{0,64},{4,68},{8,72},{12,76},{16,80},{20,84},{24,88},{28,92},{32,9... | collective-permute-start | bytes 786440 | tf_op jit(solution)/shard_map/ppermute | solution.py:17
  143.4 10.2 %collective-permute-start.17 = (f32[8,64,128]{2,1,0:T(8,128)S(1)}, f32[8,64,128]{2,1,0:T(8,128)S(1)}, u32[]{:S(2)}, u32[]{:S(2)}) collective-permute-start(f32[8,64,128]{2,1,0:T(8,128)S(1)} %multiply_add_fusion), channel_id=1, source_target_pairs={{0,64},{4,68},{8,72},{12,76},{16,80},{20,84},{24,88},{28,92},{32,9... | collective-permute-start | bytes 786440 | tf_op jit(solution)/shard_map/ppermute | solution.py:17
  155.1 15.5 %collective-permute-start.19 = (f32[16,64,128]{2,1,0:T(8,128)}, f32[16,64,128]{2,1,0:T(8,128)}, u32[]{:S(2)}, u32[]{:S(2)}) collective-permute-start(f32[16,64,128]{2,1,0:T(8,128)} %get-tuple-element.31), channel_id=1, source_target_pairs={{0,4},{4,0},{8,12},{12,8},{16,20},{20,16},{24,28},{28,24},{32,36},... | collective-permute-start | bytes 1572872 | tf_op jit(solution)/shard_map/ppermute | solution.py:175
  167.9 4.2 %copy-start.7 = (f32[2,16,64,128]{3,0,2,1:T(2,128)S(1)}, f32[2,16,64,128]{3,0,2,1:T(2,128)}, u32[]{:S(2)}) copy-start(f32[2,16,64,128]{3,0,2,1:T(2,128)} %get-tuple-element.52) | copy-start | bytes 3145732
  (9 other events, 19.8 us)
Sparse Core Ops, SparseCore 0:
  9.0 51.2 all-gather.1
where the time goes:
time: 196 us
  waiting for transfers between devices  75.5 us (39%)
  local copies, waits for them, and re-layouts  35.3 us (18%)
  matrix products  30.7 us (16%)
  starting transfers between devices  25.8 us (13%)
  other arithmetic  14.2 us (7%)
  between operations  14.1 us (7%)
    ppermute x17, waiting for transfers between devices, from_behind(): return lax.ppermute(value, axis, pairs)  39.6 us
    all_gather x1, waiting for transfers between devices, per_device(): piece = lax.all_gather(hidden, 'mp', axis=1, tiled=True)  34.1 us
    unnamed x44, local copies, waits for them, and re-layouts  19.5 us
    dot_general x1, matrix products, per_device(): zx_sum = jnp.dot(piece, flat_zx, preferred_element_type=jnp.float32)  15.8 us
    ppermute x17, starting transfers between devices, from_behind(): return lax.ppermute(value, axis, pairs)  14.1 us
    ppermute x1, starting transfers between devices, per_device(): lax.ppermute(jnp.where(core == 0, after_early, before_chip), 'seq', pair)  10.9 us
    reshape x2, local copies, waits for them, and re-layouts, per_device(): y_total.reshape(rows_dev, inner_dev) * jax.nn.silu(gate.astype(jnp.float32))  7.29 us
    dot_general x1, matrix products, per_device(): jnp.einsum('cr,rhpn->chpn', pick, state_bank, precision=lax.Precision.HIG...  4.63 us
  transfers between devices with their start and end apart: 21, of which 13 were waited for; matrix products, arithmetic and copies ran while one was open for 21% of the time, Pallas kernels for 0%

commit v1 on v0

--- a/solution.py
+++ b/solution.py
@@ -1,3 +1,4 @@
+import functools
 import jax
 import jax.numpy as jnp
 from jax import lax
@@ -9,6 +10,41 @@
 BLOCK = 256
 KERNEL = 4
 BANK = 2
+
+
+def samples_lead(local_x, chip_axis):
+    block_last, back, kept_arr = (
+        lax.axis_size(chip_axis),
+        lax.axis_index(chip_axis),
+        local_x.shape[1],
+    )
+    z1 = w_next = local_x
+    t = 1
+    v_now = lax.dynamic_update_slice_in_dim(
+        jnp.zeros(
+            [j0 * block_last if h == 1 else j0 for h, j0 in enumerate(local_x.shape)], local_x.dtype
+        ),
+        local_x,
+        back * kept_arr,
+        axis=1,
+    )
+    while t < block_last // 2 + 1:
+        z1 = lax.ppermute(z1, chip_axis, [(h, (h + 1) % block_last) for h in range(block_last)])
+        v_now = lax.dynamic_update_slice_in_dim(
+            v_now, z1, (back - t) % block_last * kept_arr, axis=1
+        )
+        if 2 * t < block_last:
+            w_next = lax.ppermute(
+                w_next, chip_axis, [(h, (h - 1) % block_last) for h in range(block_last)]
+            )
+            v_now = lax.dynamic_update_slice_in_dim(
+                v_now, w_next, (back + t) % block_last * kept_arr, axis=1
+            )
+        t += 1
+    return v_now
+
+
+notes_compute = functools.partial(samples_lead, chip_axis="mp")
 
 
 def from_behind(value, axis, steps):
@@ -54,7 +90,7 @@
     prompts = prompt_blocks.shape[0]
     flat_zx = w_zx.reshape(WIDTH, 2 * inner_dev)
     flat_bc = w_bc.reshape(WIDTH, 2 * gstate_dev)
-    piece = lax.all_gather(hidden, "mp", axis=1, tiled=True)
+    piece = notes_compute(hidden)
     zx_sum = jnp.dot(piece, flat_zx, preferred_element_type=jnp.float32)
     bc_sum = jnp.dot(piece, flat_bc, preferred_element_type=jnp.float32)
     dt_raw = jnp.dot(piece, w_dt, preferred_element_type=jnp.float32)

time: 196 us -> 184 us (0.939)
  between operations: 14.1 us -> 0.77 us
  waiting for transfers between devices: 75.5 us -> 71.6 us
  local copies, waits for them, and re-layouts: 35.3 us -> 38.3 us
  starting transfers between devices: 25.8 us -> 28.1 us
    all_gather x1 -> x0, waiting for transfers between devices: 34.1 us -> none  [per_device(): piece = lax.all_gather(hidden, 'mp', axis=1, tiled=True)]
    ppermute x0 -> x3, waiting for transfers between devices: none -> 26.4 us  [the longest x2 26.4 us: samples_lead(): lax.ppermute(z1, chip_axis, [(h, (h + 1) % block_last) for h in range(blo...]
    ppermute x17, waiting for transfers between devices: 39.6 us -> 45.1 us  [from_behind(): return lax.ppermute(value, axis, pairs)]
    ppermute x17, starting transfers between devices: 14.1 us -> 9.03 us  [from_behind(): return lax.ppermute(value, axis, pairs)]
    ppermute x2, starting transfers between devices: 0.8 us -> 5.2 us  [per_device(): lax.ppermute((keep(step_a, 1 - core), keep(step_b, 1 - core)), 'seq', pair)]
    ppermute x0 -> x3, starting transfers between devices: none -> 3.63 us  [the longest x2 2.12 us: samples_lead(): lax.ppermute(z1, chip_axis, [(h, (h + 1) % block_last) for h in range(blo...]
    unnamed x44 -> x48, local copies, waits for them, and re-layouts: 19.5 us -> 20.2 us
  transfers between devices with their start and end apart: 21 -> 23, of which waited for: 13 -> 12; matrix products, arithmetic and copies ran while one was open for 21% -> 31% of each run, Pallas kernels for 0% -> 0%
where the time goes in v1:
time: 184 us; the launch traced here: 183 us
  waiting for transfers between devices  71.6 us (39%)
  local copies, waits for them, and re-layouts  38.3 us (21%)
  matrix products  30.6 us (17%)
  starting transfers between devices  28.1 us (15%)
  other arithmetic  14.1 us (8%)
    ppermute x17, waiting for transfers between devices, from_behind(): return lax.ppermute(value, axis, pairs)  45.1 us
    ppermute x2, waiting for transfers between devices, samples_lead(): lax.ppermute(z1, chip_axis, [(h, (h + 1) % block_last) for h in range(blo...  26.4 us
    unnamed x48, local copies, waits for them, and re-layouts  20.2 us
    dot_general x1, matrix products, per_device(): zx_sum = jnp.dot(piece, flat_zx, preferred_element_type=jnp.float32)  15.7 us
    ppermute x1, starting transfers between devices, per_device(): lax.ppermute(jnp.where(core == 0, after_early, before_chip), 'seq', pair)  10.2 us
    ppermute x17, starting transfers between devices, from_behind(): return lax.ppermute(value, axis, pairs)  9.03 us
    reshape x2, local copies, waits for them, and re-layouts, per_device(): y_total.reshape(rows_dev, inner_dev) * jax.nn.silu(gate.astype(jnp.float32))  7.28 us
    ppermute x2, starting transfers between devices, per_device(): lax.ppermute((keep(step_a, 1 - core), keep(step_b, 1 - core)), 'seq', pair)  5.2 us
  transfers between devices with their start and end apart: 23, of which 12 were waited for; matrix products, arithmetic and copies ran while one was open for 31% of the time, Pallas kernels for 0%

profile of v1, /device:TPU:1, one launch (start us, length us, event | category | flops | bytes accessed | tf_op | source)
XLA Modules:
  0.0 183.4 jit_solution(14752957720986038420)
XLA Ops:
  0.0 2.1 %collective-permute-start = (bf16[512,1024]{1,0:T(8,128)(2,1)}, bf16[512,1024]{1,0:T(8,128)(2,1)S(1)}, u32[]{:S(2)}, u32[]{:S(2)}) collective-permute-start(bf16[512,1024]{1,0:T(8,128)(2,1)} %param.18), channel_id=1, source_target_pairs={{0,1},{1,2},{2,3},{3,0},{4,5},{5,6},{6,7},{7,4},{8,9},{9,10},{10,1... | collective-permute-start | bytes 3145736 | tf_op jit(solution)/shard_map/ppermute | solution.py:32
  2.1 1.5 collective-permute-start.1
  4.7 17.1 %copy.111 = bf16[512,8,2,1024]{3,1,2,0:T(8,128)(2,1)} copy(bf16[512,8,2,1024]{3,2,1,0:T(2,128)(2,1)} %bitcast.142) | data formatting | bytes 33554432
  22.3 4.2 %collective-permute-done = bf16[512,1024]{1,0:T(8,128)(2,1)S(1)} collective-permute-done((bf16[512,1024]{1,0:T(8,128)(2,1)}, bf16[512,1024]{1,0:T(8,128)(2,1)S(1)}, u32[]{:S(2)}, u32[]{:S(2)}) %collective-permute-start) | collective-permute-done | bytes 1048608 | tf_op jit(solution)/shard_map/ppermute | solution.py:32
  28.9 22.2 %collective-permute-done.2 = bf16[512,1024]{1,0:T(8,128)(2,1)S(1)} collective-permute-done((bf16[512,1024]{1,0:T(8,128)(2,1)S(1)}, bf16[512,1024]{1,0:T(8,128)(2,1)S(1)}, u32[]{:S(2)}, u32[]{:S(2)}) %collective-permute-start.2) | collective-permute-done | bytes 1048608 | tf_op jit(solution)/shard_map/ppermute | solution.py:32
  51.2 1.9 %copy-done.1 = bf16[512,4096]{1,0:T(8,128)(2,1)} copy-done((bf16[512,4096]{1,0:T(8,128)(2,1)}, bf16[512,4096]{1,0:T(8,128)(2,1)S(1)}, u32[]{:S(2)}) %copy-start.1) | copy-done | bytes 4194328
  56.4 2.2 %collective-permute-start.4 = (f32[16]{0:T(128)S(1)}, f32[16]{0:T(128)S(1)}, u32[]{:S(2)}, u32[]{:S(2)}) collective-permute-start(f32[16]{0:T(128)S(1)} %reshape.274), channel_id=1, source_target_pairs={{0,4},{4,0},{8,12},{12,8},{16,20},{20,16},{24,28},{28,24},{32,36},... | collective-permute-start | bytes 200 | tf_op jit(solution)/shard_map/ppermute | solution.py:169
  58.7 15.7 %convolution_convert_fusion = bf16[512,2048]{1,0:T(8,128)(2,1)S(1)} fusion(bf16[512,4096]{1,0:T(8,128)(2,1)} %copy-done.1, bf16[4096,2048]{1,0:T(8,128)(2,1)} %bitcast.143), kind=kOutput, calls=%fused_computation.8 | convolution fusion | flops 8590983168 | bytes 23068672 | tf_op jit(solution)/shard_map/dot_general | solution.py:94
  77.8 1.6 collective-permute-start.5
  81.4 1.7 multiply_convert_fusion.2
  85.5 2.3 %copy.84 = bf16[2,256,1024]{1,2,0:T(8,128)(2,1)} copy(bf16[2,256,1024]{2,1,0:T(8,128)(2,1)} %get-tuple-element.33) | data formatting | bytes 2097152 | tf_op jit(solution)/shard_map/slice | solution.py:131
  87.7 1.7 fusion.23
  89.4 4.6 %copy_add_fusion = (f32[2,16,64,128]{3,0,2,1:T(2,128)S(1)}, f32[2,16,64,128]{3,0,2,1:T(2,128)}) fusion(f32[2,16,64,128]{3,2,1,0:T(8,128)S(1)} %fusion.23, pred[2]{0:T(512)(128)(4,1)S(1)} %compare_reduce_fusion, f32[2,16]{0,1:T(8,128)S(1)} %copy.89, f32[2,16,64,128]{3,2,1,0:T(8,128)S(1)} %copy-done, s32[2]{0:T(128)S(1)} %fusion.46), kind=kOutput, calls=%fused_computation.42 | convolution fusion | flops 7077892 | bytes 4194442 | tf_op jit(solution)/shard_map/cr,rhpn->chpn/dot_general | solution.py:118
  94.2 3.0 %collective-permute-start.8 = (f32[16,64,128]{2,1,0:T(8,128)S(1)}, f32[16,64,128]{2,1,0:T(8,128)S(1)}, u32[]{:S(2)}, u32[]{:S(2)}) collective-permute-start(f32[16,64,128]{2,1,0:T(8,128)S(1)} %bitcast.155), channel_id=1, source_target_pairs={{0,4},{4,0},{8,12},{12,8},{16,20},{20,16},{24,28},{28,24},{32,36},... | collective-permute-start | bytes 1572872 | tf_op jit(solution)/shard_map/ppermute | solution.py:169
  97.4 1.7 collective-permute-start.15
  99.0 4.3 %collective-permute-done.6 = f32[8]{0:T(128)S(1)} collective-permute-done((f32[8]{0:T(128)S(1)}, f32[8]{0:T(128)S(1)}, u32[]{:S(2)}, u32[]{:S(2)}) %collective-permute-start.6) | collective-permute-done | bytes 64 | tf_op jit(solution)/shard_map/ppermute | solution.py:53
  103.8 3.2 %collective-permute-done.7 = f32[8]{0:T(128)S(1)} collective-permute-done((f32[8]{0:T(128)S(1)}, f32[8]{0:T(128)S(1)}, u32[]{:S(2)}, u32[]{:S(2)}) %collective-permute-start.7) | collective-permute-done | bytes 64 | tf_op jit(solution)/shard_map/ppermute | solution.py:53
  107.7 6.0 %collective-permute-done.9 = f32[8,64,128]{2,1,0:T(8,128)S(1)} collective-permute-done((f32[8,64,128]{2,1,0:T(8,128)S(1)}, f32[8,64,128]{2,1,0:T(8,128)S(1)}, u32[]{:S(2)}, u32[]{:S(2)}) %collective-permute-start.9) | collective-permute-done | bytes 262176 | tf_op jit(solution)/shard_map/ppermute | solution.py:53
  114.0 5.4 %collective-permute-done.17 = f32[8,64,128]{2,1,0:T(8,128)S(1)} collective-permute-done((f32[8,64,128]{2,1,0:T(8,128)S(1)}, f32[8,64,128]{2,1,0:T(8,128)S(1)}, u32[]{:S(2)}, u32[]{:S(2)}) %collective-permute-start.17) | collective-permute-done | bytes 262176 | tf_op jit(solution)/shard_map/ppermute | solution.py:53
  119.6 4.3 %collective-permute-done.10 = f32[8,64,128]{2,1,0:T(8,128)S(1)} collective-permute-done((f32[8,64,128]{2,1,0:T(8,128)S(1)}, f32[8,64,128]{2,1,0:T(8,128)S(1)}, u32[]{:S(2)}, u32[]{:S(2)}) %collective-permute-start.10) | collective-permute-done | bytes 262176 | tf_op jit(solution)/shard_map/ppermute | solution.py:53
  124.2 5.4 %collective-permute-done.18 = f32[8,64,128]{2,1,0:T(8,128)S(1)} collective-permute-done((f32[8,64,128]{2,1,0:T(8,128)S(1)}, f32[8,64,128]{2,1,0:T(8,128)S(1)}, u32[]{:S(2)}, u32[]{:S(2)}) %collective-permute-start.18) | collective-permute-done | bytes 262176 | tf_op jit(solution)/shard_map/ppermute | solution.py:53
  132.3 6.4 %collective-permute-done.19 = f32[8,64,128]{2,1,0:T(8,128)S(1)} collective-permute-done((f32[8,64,128]{2,1,0:T(8,128)S(1)}, f32[8,64,128]{2,1,0:T(8,128)S(1)}, u32[]{:S(2)}, u32[]{:S(2)}) %collective-permute-start.19) | collective-permute-done | bytes 262176 | tf_op jit(solution)/shard_map/ppermute | solution.py:53
  139.1 3.3 %collective-permute-done.12 = f32[8,64,128]{2,1,0:T(8,128)S(1)} collective-permute-done((f32[8,64,128]{2,1,0:T(8,128)S(1)}, f32[8,64,128]{2,1,0:T(8,128)S(1)}, u32[]{:S(2)}, u32[]{:S(2)}) %collective-permute-start.12) | collective-permute-done | bytes 262176 | tf_op jit(solution)/shard_map/ppermute | solution.py:53
  142.8 6.2 %collective-permute-done.20 = f32[8,64,128]{2,1,0:T(8,128)S(1)} collective-permute-done((f32[8,64,128]{2,1,0:T(8,128)S(1)}, f32[8,64,128]{2,1,0:T(8,128)S(1)}, u32[]{:S(2)}, u32[]{:S(2)}) %collective-permute-start.20) | collective-permute-done | bytes 262176 | tf_op jit(solution)/shard_map/ppermute | solution.py:53
  150.5 10.2 %collective-permute-start.22 = (f32[16,64,128]{2,1,0:T(8,128)}, f32[16,64,128]{2,1,0:T(8,128)}, u32[]{:S(2)}, u32[]{:S(2)}) collective-permute-start(f32[16,64,128]{2,1,0:T(8,128)} %get-tuple-element.31), channel_id=1, source_target_pairs={{0,4},{4,0},{8,12},{12,8},{16,20},{20,16},{24,28},{28,24},{32,36},... | collective-permute-start | bytes 1572872 | tf_op jit(solution)/shard_map/ppermute | solution.py:211
  160.7 1.8 %copy.98 = f32[2,256,1024]{1,2,0:T(8,128)} copy(f32[2,256,1024]{2,1,0:T(8,128)S(1)} %get-tuple-element.32) | data formatting | bytes 4194304 | tf_op jit(solution)/shard_map/convert_element_type | solution.py:149
  167.7 2.0 %fusion.25 = f32[2,16,64,256]{3,2,1,0:T(8,128)S(1)} fusion(f32[2,16,64,128]{3,0,2,1:T(2,128)S(1)} %fusion.24, bf16[2,256,1280]{2,1,0:T(8,128)(2,1)} %copy-done.3), kind=kOutput, calls=%fused_computation.40 | convolution fusion | flops 805306368 | bytes 3276800 | tf_op jit(solution)/shard_map/cqgn,cgjpn->cqgjp/dot_general | solution.py:220
  169.7 2.6 %fusion.19 = f32[2,256,1,16,64]{1,4,3,0,2:T(8,128)S(1)} fusion(f32[2,16,64,256]{3,2,1,0:T(8,128)S(1)} %fusion.25, f32[2,256,1,16,64]{1,4,3,0,2:T(8,128)S(1)} %bitcast.149, bf16[2,256,16,64]{1,3,2,0:T(8,128)(2,1)S(1)} %bitcast.147, f32[2,16,256]{2,1,0:T(8,128)S(1)} %get-tuple-element.42, f32[2,16,256]{2,1,0:T(8,128)S(1)} %get-tuple-element.45, ...), kind=kOutput, calls=%fused_computation.30 | convolution fusion | flops 281018368 | bytes 8028224 | tf_op jit(solution)/shard_map/cgjqk,ckgjp->cqgjp/dot_general | solution.py:145
  172.3 3.8 %copy.105 = f32[2,256,1,16,64]{4,3,1,0,2:T(8,128)} copy(f32[2,256,1,16,64]{1,4,3,0,2:T(8,128)S(1)} %fusion.19) | data formatting | bytes 4194304 | tf_op jit(solution)/shard_map/reshape | solution.py:229
  176.1 3.5 %reshape.290 = f32[512,1024]{1,0:T(8,128)S(1)} reshape(f32[2,256,1,16,64]{4,3,1,0,2:T(8,128)} %copy.105) | data formatting | bytes 4194304 | tf_op jit(solution)/shard_map/reshape | solution.py:229
  179.6 2.1 %multiply_reduce_fusion = f32[512]{0:T(512)S(1)} fusion(f32[512,1024]{1,0:T(8,128)S(1)} %reshape.290, bf16[512,2048]{1,0:T(8,128)(2,1)} %copy-done.4), kind=kLoop, calls=%fused_computation.32 | loop fusion | flops 4193792 | bytes 3147776 | tf_op jit(solution)/shard_map/reduce_sum | solution.py:231
  181.7 1.7 multiply_convert_fusion.3
  (160 shorter events, 26.9 us)
Async XLA Ops:
  0.0 89.4 %copy-start = (f32[2,16,64,128]{3,2,1,0:T(8,128)S(1)}, f32[2,16,64,128]{3,2,1,0:T(8,128)}, u32[]{:S(2)}) copy-start(f32[2,16,64,128]{3,2,1,0:T(8,128)} %param.30) | copy-start | bytes 3145732
  0.0 26.5 %collective-permute-start = (bf16[512,1024]{1,0:T(8,128)(2,1)}, bf16[512,1024]{1,0:T(8,128)(2,1)S(1)}, u32[]{:S(2)}, u32[]{:S(2)}) collective-permute-start(bf16[512,1024]{1,0:T(8,128)(2,1)} %param.18), channel_id=1, source_target_pairs={{0,1},{1,2},{2,3},{3,0},{4,5},{5,6},{6,7},{7,4},{8,9},{9,10},{10,1... | collective-permute-start | bytes 3145736 | tf_op jit(solution)/shard_map/ppermute | solution.py:32
  2.1 25.3 %collective-permute-start.1 = (bf16[512,1024]{1,0:T(8,128)(2,1)}, bf16[512,1024]{1,0:T(8,128)(2,1)}, u32[]{:S(2)}, u32[]{:S(2)}) collective-permute-start(bf16[512,1024]{1,0:T(8,128)(2,1)} %param.18), channel_id=1, source_target_pairs={{0,3},{1,0},{2,1},{3,2},{4,7},{5,4},{6,5},{7,6},{8,11},{9,8},{10,9... | collective-permute-start | bytes 3145736 | tf_op jit(solution)/shard_map/ppermute | solution.py:37
  4.7 17.1 %copy-start.15 = (bf16[2,3,2,128]{3,2,1,0:T(2,128)(2,1)S(1)}, bf16[2,3,2,128]{3,2,1,0:T(2,128)(2,1)}, u32[]{:S(2)}) copy-start(bf16[2,3,2,128]{3,2,1,0:T(2,128)(2,1)} %param.32) | copy-start | bytes 9220
  4.7 17.6 %copy-start.11 = (f32[4,1024]{1,0:T(4,128)S(1)}, f32[4,1024]{1,0:T(4,128)}, u32[]{:S(2)}) copy-start(f32[4,1024]{1,0:T(4,128)} %param.22) | copy-start | bytes 49156
  4.7 21.8 %copy-start.13 = (f32[1024]{0:T(1024)S(1)}, f32[1024]{0:T(1024)}, u32[]{:S(2)}) copy-start(f32[1024]{0:T(1024)} %param.23) | copy-start | bytes 12292
  4.7 21.8 %copy-start.17 = (f32[2,128]{1,0:T(2,128)S(1)}, f32[2,128]{1,0:T(2,128)}, u32[]{:S(2)}) copy-start(f32[2,128]{1,0:T(2,128)} %param.25) | copy-start | bytes 3076
  4.7 21.8 %copy-start.14 = (f32[4,2,128]{2,1,0:T(2,128)S(1)}, f32[4,2,128]{2,1,0:T(2,128)}, u32[]{:S(2)}) copy-start(f32[4,2,128]{2,1,0:T(2,128)} %param.24) | copy-start | bytes 12292
  26.5 24.6 %collective-permute-start.2 = (bf16[512,1024]{1,0:T(8,128)(2,1)S(1)}, bf16[512,1024]{1,0:T(8,128)(2,1)S(1)}, u32[]{:S(2)}, u32[]{:S(2)}) collective-permute-start(bf16[512,1024]{1,0:T(8,128)(2,1)S(1)} %collective-permute-done), channel_id=1, source_target_pairs={{0,1},{1,2},{2,3},{3,0},{4,5},{5,6},{6,7},{7,4},{8,9},{9,10},{10,1... | collective-permute-start | bytes 3145736 | tf_op jit(solution)/shard_map/ppermute | solution.py:32
  27.4 25.7 %copy-start.10 = (bf16[4096,16]{0,1:T(8,128)(2,1)S(1)}, bf16[4096,16]{0,1:T(8,128)(2,1)}, u32[]{:S(2)}) copy-start(bf16[4096,16]{0,1:T(8,128)(2,1)} %param.21) | copy-start | bytes 393220
  56.4 21.2 %collective-permute-start.4 = (f32[16]{0:T(128)S(1)}, f32[16]{0:T(128)S(1)}, u32[]{:S(2)}, u32[]{:S(2)}) collective-permute-start(f32[16]{0:T(128)S(1)} %reshape.274), channel_id=1, source_target_pairs={{0,4},{4,0},{8,12},{12,8},{16,20},{20,16},{24,28},{28,24},{32,36},... | collective-permute-start | bytes 200 | tf_op jit(solution)/shard_map/ppermute | solution.py:169
  58.7 15.9 %copy-start.2 = (bf16[512,4096]{1,0:T(8,128)(2,1)S(1)}, bf16[512,4096]{1,0:T(8,128)(2,1)}, u32[]{:S(2)}) copy-start(bf16[512,4096]{1,0:T(8,128)(2,1)} %copy-done.1) | copy-start | bytes 12582916
  58.7 15.9 %copy-start.18 = (bf16[4096,2,128]{2,1,0:T(2,128)(2,1)S(1)}, bf16[4096,2,128]{2,1,0:T(2,128)(2,1)}, u32[]{:S(2)}) copy-start(bf16[4096,2,128]{2,1,0:T(2,128)(2,1)} %param.20) | copy-start | bytes 6291460
  76.0 4.8 %collective-permute-start.3 = (bf16[2,3,1280]{2,0,1:T(2,128)(2,1)S(1)}, bf16[2,3,1280]{2,0,1:T(2,128)(2,1)S(1)}, u32[]{:S(2)}, u32[]{:S(2)}) collective-permute-start(bf16[2,3,1280]{2,0,1:T(2,128)(2,1)S(1)} %copy.107), channel_id=1, source_target_pairs={{0,4},{4,8},{8,12},{12,16},{16,20},{20,24},{24,28},{28,32},{32,36}... | collective-permute-start | bytes 46088 | tf_op jit(solution)/shard_map/ppermute | solution.py:53
  77.8 19.4 %collective-permute-start.5 = (f32[8]{0:T(128)S(1)}, f32[8]{0:T(128)S(1)}, u32[]{:S(2)}, u32[]{:S(2)}) collective-permute-start(f32[8]{0:T(128)S(1)} %reshape_squeeze.12), channel_id=1, source_target_pairs={{0,8},{4,12},{8,16},{12,20},{16,24},{20,28},{24,32},{28,36},{32,40... | collective-permute-start | bytes 104 | tf_op jit(solution)/shard_map/ppermute | solution.py:53
  79.5 17.7 %collective-permute-start.14 = (f32[8]{0:T(128)S(1)}, f32[8]{0:T(128)S(1)}, u32[]{:S(2)}, u32[]{:S(2)}) collective-permute-start(f32[8]{0:T(128)S(1)} %reshape_squeeze.14), channel_id=1, source_target_pairs={{0,8},{4,12},{8,16},{12,20},{16,24},{20,28},{24,32},{28,36},{32,40... | collective-permute-start | bytes 104 | tf_op jit(solution)/shard_map/ppermute | solution.py:53
  94.2 9.2 %collective-permute-start.8 = (f32[16,64,128]{2,1,0:T(8,128)S(1)}, f32[16,64,128]{2,1,0:T(8,128)S(1)}, u32[]{:S(2)}, u32[]{:S(2)}) collective-permute-start(f32[16,64,128]{2,1,0:T(8,128)S(1)} %bitcast.155), channel_id=1, source_target_pairs={{0,4},{4,0},{8,12},{12,8},{16,20},{20,16},{24,28},{28,24},{32,36},... | collective-permute-start | bytes 1572872 | tf_op jit(solution)/shard_map/ppermute | solution.py:169
  97.2 6.0 %collective-permute-start.6 = (f32[8]{0:T(128)S(1)}, f32[8]{0:T(128)S(1)}, u32[]{:S(2)}, u32[]{:S(2)}) collective-permute-start(f32[8]{0:T(128)S(1)} %get-tuple-element.18), channel_id=1, source_target_pairs={{0,16},{4,20},{8,24},{12,28},{16,32},{20,36},{24,40},{28,44},{32,4... | collective-permute-start | bytes 104 | tf_op jit(solution)/shard_map/ppermute | solution.py:53
  97.4 6.4 %collective-permute-start.15 = (f32[8]{0:T(128)S(1)}, f32[8]{0:T(128)S(1)}, u32[]{:S(2)}, u32[]{:S(2)}) collective-permute-start(f32[8]{0:T(128)S(1)} %get-tuple-element.25), channel_id=1, source_target_pairs={{0,16},{4,20},{8,24},{12,28},{16,32},{20,36},{24,40},{28,44},{32,4... | collective-permute-start | bytes 104 | tf_op jit(solution)/shard_map/ppermute | solution.py:53
  103.4 3.6 %collective-permute-start.7 = (f32[8]{0:T(128)S(1)}, f32[8]{0:T(128)S(1)}, u32[]{:S(2)}, u32[]{:S(2)}) collective-permute-start(f32[8]{0:T(128)S(1)} %fusion.58), channel_id=1, source_target_pairs={{0,32},{4,36},{8,40},{12,44},{16,48},{20,52},{24,56},{28,60},{32,6... | collective-permute-start | bytes 104 | tf_op jit(solution)/shard_map/ppermute | solution.py:53
  103.6 10.1 %collective-permute-start.9 = (f32[8,64,128]{2,1,0:T(8,128)S(1)}, f32[8,64,128]{2,1,0:T(8,128)S(1)}, u32[]{:S(2)}, u32[]{:S(2)}) collective-permute-start(f32[8,64,128]{2,1,0:T(8,128)S(1)} %bitcast.154), channel_id=1, source_target_pairs={{0,8},{4,12},{8,16},{12,20},{16,24},{20,28},{24,32},{28,36},{32,40... | collective-permute-start | bytes 786440 | tf_op jit(solution)/shard_map/ppermute | solution.py:53
  103.8 10.1 %collective-permute-start.16 = (f32[8]{0:T(128)S(1)}, f32[8]{0:T(128)S(1)}, u32[]{:S(2)}, u32[]{:S(2)}) collective-permute-start(f32[8]{0:T(128)S(1)} %fusion.60), channel_id=1, source_target_pairs={{0,32},{4,36},{8,40},{12,44},{16,48},{20,52},{24,56},{28,60},{32,6... | collective-permute-start | bytes 104 | tf_op jit(solution)/shard_map/ppermute | solution.py:53
  107.1 17.0 %collective-permute-start.13 = (f32[8]{0:T(128)S(1)}, f32[8]{0:T(128)S(1)}, u32[]{:S(2)}, u32[]{:S(2)}) collective-permute-start(f32[8]{0:T(128)S(1)} %fusion.53), channel_id=1, source_target_pairs={{0,64},{4,68},{8,72},{12,76},{16,80},{20,84},{24,88},{28,92},{32,9... | collective-permute-start | bytes 104 | tf_op jit(solution)/shard_map/ppermute | solution.py:53
  107.7 11.7 %collective-permute-start.17 = (f32[8,64,128]{2,1,0:T(8,128)S(1)}, f32[8,64,128]{2,1,0:T(8,128)S(1)}, u32[]{:S(2)}, u32[]{:S(2)}) collective-permute-start(f32[8,64,128]{2,1,0:T(8,128)S(1)} %bitcast.153), channel_id=1, source_target_pairs={{0,8},{4,12},{8,16},{12,20},{16,24},{20,28},{24,32},{28,36},{32,40... | collective-permute-start | bytes 786440 | tf_op jit(solution)/shard_map/ppermute | solution.py:53
  113.8 10.1 %collective-permute-start.10 = (f32[8,64,128]{2,1,0:T(8,128)S(1)}, f32[8,64,128]{2,1,0:T(8,128)S(1)}, u32[]{:S(2)}, u32[]{:S(2)}) collective-permute-start(f32[8,64,128]{2,1,0:T(8,128)S(1)} %multiply_add_fusion.5), channel_id=1, source_target_pairs={{0,16},{4,20},{8,24},{12,28},{16,32},{20,36},{24,40},{28,44},{32,4... | collective-permute-start | bytes 786440 | tf_op jit(solution)/shard_map/ppermute | solution.py:53
  114.0 18.1 %collective-permute-start.21 = (f32[8]{0:T(128)S(1)}, f32[8]{0:T(128)S(1)}, u32[]{:S(2)}, u32[]{:S(2)}) collective-permute-start(f32[8]{0:T(128)S(1)} %fusion.55), channel_id=1, source_target_pairs={{0,64},{4,68},{8,72},{12,76},{16,80},{20,84},{24,88},{28,92},{32,9... | collective-permute-start | bytes 104 | tf_op jit(solution)/shard_map/ppermute | solution.py:53
  119.5 10.1 %collective-permute-start.18 = (f32[8,64,128]{2,1,0:T(8,128)S(1)}, f32[8,64,128]{2,1,0:T(8,128)S(1)}, u32[]{:S(2)}, u32[]{:S(2)}) collective-permute-start(f32[8,64,128]{2,1,0:T(8,128)S(1)} %multiply_add_fusion.2), channel_id=1, source_target_pairs={{0,16},{4,20},{8,24},{12,28},{16,32},{20,36},{24,40},{28,44},{32,4... | collective-permute-start | bytes 786440 | tf_op jit(solution)/shard_map/ppermute | solution.py:53
  124.0 6.5 %collective-permute-start.11 = (f32[8,64,128]{2,1,0:T(8,128)S(1)}, f32[8,64,128]{2,1,0:T(8,128)S(1)}, u32[]{:S(2)}, u32[]{:S(2)}) collective-permute-start(f32[8,64,128]{2,1,0:T(8,128)S(1)} %multiply_add_fusion.4), channel_id=1, source_target_pairs={{0,32},{4,36},{8,40},{12,44},{16,48},{20,52},{24,56},{28,60},{32,6... | collective-permute-start | bytes 786440 | tf_op jit(solution)/shard_map/ppermute | solution.py:53
  129.7 9.0 %collective-permute-start.19 = (f32[8,64,128]{2,1,0:T(8,128)S(1)}, f32[8,64,128]{2,1,0:T(8,128)S(1)}, u32[]{:S(2)}, u32[]{:S(2)}) collective-permute-start(f32[8,64,128]{2,1,0:T(8,128)S(1)} %multiply_add_fusion.1), channel_id=1, source_target_pairs={{0,32},{4,36},{8,40},{12,44},{16,48},{20,52},{24,56},{28,60},{32,6... | collective-permute-start | bytes 786440 | tf_op jit(solution)/shard_map/ppermute | solution.py:53
  130.6 11.8 %collective-permute-start.12 = (f32[8,64,128]{2,1,0:T(8,128)S(1)}, f32[8,64,128]{2,1,0:T(8,128)S(1)}, u32[]{:S(2)}, u32[]{:S(2)}) collective-permute-start(f32[8,64,128]{2,1,0:T(8,128)S(1)} %multiply_add_fusion.3), channel_id=1, source_target_pairs={{0,64},{4,68},{8,72},{12,76},{16,80},{20,84},{24,88},{28,92},{32,9... | collective-permute-start | bytes 786440 | tf_op jit(solution)/shard_map/ppermute | solution.py:53
  138.8 10.1 %collective-permute-start.20 = (f32[8,64,128]{2,1,0:T(8,128)S(1)}, f32[8,64,128]{2,1,0:T(8,128)S(1)}, u32[]{:S(2)}, u32[]{:S(2)}) collective-permute-start(f32[8,64,128]{2,1,0:T(8,128)S(1)} %multiply_add_fusion), channel_id=1, source_target_pairs={{0,64},{4,68},{8,72},{12,76},{16,80},{20,84},{24,88},{28,92},{32,9... | collective-permute-start | bytes 786440 | tf_op jit(solution)/shard_map/ppermute | solution.py:53
  150.5 14.8 %collective-permute-start.22 = (f32[16,64,128]{2,1,0:T(8,128)}, f32[16,64,128]{2,1,0:T(8,128)}, u32[]{:S(2)}, u32[]{:S(2)}) collective-permute-start(f32[16,64,128]{2,1,0:T(8,128)} %get-tuple-element.31), channel_id=1, source_target_pairs={{0,4},{4,0},{8,12},{12,8},{16,20},{20,16},{24,28},{28,24},{32,36},... | collective-permute-start | bytes 1572872 | tf_op jit(solution)/shard_map/ppermute | solution.py:211
  (13 other events, 33.6 us)
